TPU v7x, 256 devices: a whole 4x4x8 slice. The times are simulated.
256 devices in a mesh: seq: 64 (over z, x, core), head: 4 (over y).
Axes of the slice: x: 4, y: 4, z: 8, core: 2. Of those that a mesh axis runs over, the one named last changes fastest.
Arguments:
- features: bfloat16 [8192, 4096], P('seq', 'head'), may hold values from -6 to 6
- proj_weight: bfloat16 [4096, 4096], P(None, 'head'), may hold values from -0.09375 to 0.09375
- query_vectors: bfloat16 [8192, 4096], P('seq', 'head'), may hold values from -6 to 6
- key_vectors: bfloat16 [8192, 4096], P('seq', 'head'), may hold values from -6 to 6
Outputs:
- rotated_queries: bfloat16 [8192, 4096], P('seq', 'head')
- rotated_keys: bfloat16 [8192, 4096], P('seq', 'head')
All inputs are finite; a program needn't handle non-finite values.
Results may differ from a plain program's by a relative error of at most 0.0024.
Values may be sent and summed in bfloat16 or wider, within the bound.
No kernel may reach another device: no remote copies, remote signals or barrier semaphores. Data moves between devices by JAX's collectives and lax.ppermute only.
A program may use at most 128 MiB of HBM per device.

v0:
```python
import jax
import jax.numpy as jnp
from jax import lax
from jax.sharding import PartitionSpec as P

HEAD_DIM = 128


def entering(array, axis, combine, identity):
    count, place = (lax.axis_size(axis), lax.axis_index(axis))
    everything = lax.all_gather(array, axis)
    start = jnp.broadcast_to(jnp.asarray(identity, array.dtype), array.shape)

    def turn(k, before):
        reached = k < place
        new = combine(before, everything[k])
        return jnp.where(reached, new, before)

    return lax.fori_loop(0, count, turn, start)


def small_inverse(matrix):
    highest = lax.Precision.HIGHEST
    size = matrix.shape[-1]
    position = jnp.arange(size)
    strict = (position[:, None] < position[None, :]).astype(jnp.float32)
    eye_block = jnp.eye(size, dtype=jnp.float32)
    power = -2.0 * matrix * strict[None]
    result = eye_block[None] + power
    reach = 2
    while reach < size:
        power = jnp.einsum("hij,hjk->hik", power, power, precision=highest)
        result = result + jnp.einsum("hij,hjk->hik", result, power, precision=highest)
        reach = reach * 2
    return 2.0 * result


def triangle_inverse(matrix):
    highest = lax.Precision.HIGHEST
    size = matrix.shape[-1]
    if size <= 16:
        return small_inverse(matrix)
    half = size // 2
    first = triangle_inverse(matrix[:, :half, :half])
    second = triangle_inverse(matrix[:, half:, half:])
    coupling = matrix[:, :half, half:]
    middle = jnp.einsum("hij,hjk->hik", first, coupling, precision=highest)
    corner = -jnp.einsum("hij,hjk->hik", middle, second, precision=highest)
    lower_left = jnp.zeros((matrix.shape[0], size - half, half), jnp.float32)
    top = jnp.concatenate([first, corner], axis=2)
    bottom = jnp.concatenate([lower_left, second], axis=2)
    return jnp.concatenate([top, bottom], axis=1)


def upper_solve(matrix, right_side):
    highest = lax.Precision.HIGHEST
    rows = matrix.shape[1]
    size = min(128, rows)
    count = rows // size
    solved_blocks = []
    for i in reversed(range(count)):
        inverse_block = triangle_inverse(matrix)
        solved_blocks.append(
            jnp.einsum("hij,hjk->hik", inverse_block, right_side, precision=highest)
        )
    return jnp.concatenate(solved_blocks[::-1], axis=1)


def body(features, proj_weight, query_vectors, key_vectors):
    highest = lax.Precision.HIGHEST
    tok_rows = query_vectors.shape[0]
    width = proj_weight.shape[1]
    local_heads = width // HEAD_DIM
    raw_proj = jnp.dot(
        lax.all_gather(features, "head", axis=1, tiled=True),
        proj_weight,
        preferred_element_type=jnp.float32,
    )
    raw_proj = raw_proj.reshape(tok_rows, local_heads, HEAD_DIM)
    directions = raw_proj * lax.rsqrt(jnp.sum(raw_proj * raw_proj, axis=-1, keepdims=True) + 1e-06)
    reflectors = jnp.transpose(directions, (1, 0, 2))
    targets = jnp.concatenate(
        [
            query_vectors.reshape(tok_rows, local_heads, HEAD_DIM),
            key_vectors.reshape(tok_rows, local_heads, HEAD_DIM),
        ],
        axis=0,
    )
    targets = jnp.transpose(targets.astype(jnp.float32), (1, 0, 2))
    gram = jnp.einsum("hid,hjd->hij", reflectors, reflectors, precision=highest)
    position = jnp.arange(tok_rows)
    upper = (position[:, None] < position[None, :]).astype(jnp.float32)
    identity_tok = jnp.eye(tok_rows, dtype=jnp.float32)
    inverse_t = gram * upper[None] + 0.5 * identity_tok[None]
    projected = jnp.einsum("hid,htd->hit", reflectors, targets, precision=highest)
    target_pos = jnp.concatenate([position, position])
    keep = (position[:, None] <= target_pos[None, :]).astype(jnp.float32)
    masked = projected * keep[None]
    right_side = jnp.concatenate([masked, reflectors], axis=2)
    solved = upper_solve(inverse_t, right_side)
    weights_tok = solved[:, :, : 2 * tok_rows]
    factor = solved[:, :, 2 * tok_rows :]
    local_part = targets - jnp.einsum("hit,hid->htd", weights_tok, reflectors, precision=highest)
    identity = jnp.broadcast_to(
        jnp.eye(HEAD_DIM, dtype=jnp.float32), (local_heads, HEAD_DIM, HEAD_DIM)
    )
    block_product = identity - jnp.einsum("hid,hie->hde", reflectors, factor, precision=highest)

    def combine(earlier, later):
        return jnp.einsum("hde,hef->hdf", earlier, later, precision=highest)

    carried = entering(block_product, "seq", combine, identity)
    rotated = jnp.einsum("hde,hte->htd", carried, local_part, precision=highest)
    rotated = jnp.transpose(rotated, (1, 0, 2))
    rotated_queries = rotated[:tok_rows].reshape(tok_rows, width).astype(jnp.bfloat16)
    rotated_keys = rotated[tok_rows:].reshape(tok_rows, width).astype(jnp.bfloat16)
    return (rotated_queries, rotated_keys)


def solution(mesh):
    in_specs = (P("seq", "head"), P(None, "head"), P("seq", "head"), P("seq", "head"))
    out_specs = (P("seq", "head"), P("seq", "head"))
    return jax.shard_map(body, mesh=mesh, in_specs=in_specs, out_specs=out_specs, check_vma=False)
```

profile of v0, /device:TPU:1, one launch (start us, length us, event | category | flops | bytes accessed | tf_op | source)
XLA Modules:
  0.0 355.1 jit_solution(6094807427301237134)
XLA Ops:
  10.7 27.5 %all-gather.4.cloned.1.call-done = bf16[128,4096]{1,0:T(8,128)(2,1)} async-done(((bf16[128,1024]{1,0:T(8,128)(2,1)}), bf16[128,4096]{1,0:T(8,128)(2,1)}) %all-gather.4.cloned.1.call-update) | async-done | bytes 1048592 | tf_op jit(solution)/shard_map/all_gather | solution.py:75
  38.2 5.0 %fusion.124 = f32[128,1024]{1,0:T(8,128)S(1)} fusion(bf16[128,4096]{1,0:T(8,128)(2,1)} %all-gather.4.cloned.1.call-done, bf16[4096,1024]{1,0:T(8,128)(2,1)} %param.7), kind=kOutput, calls=%fused_computation.185 | convolution fusion | flops 1073741824 | bytes 9961472 | tf_op jit(solution)/shard_map/dot_general | solution.py:74
  64.4 2.9 convolution_subtract_fusion
  67.3 141.6 %all-gather.6.cloned.1.call-done = f32[512,128,128]{2,1,0:T(8,128)} async-done(((f32[8,128,128]{2,1,0:T(8,128)}), f32[512,128,128]{2,1,0:T(8,128)}) %all-gather.6.cloned.1.call-update) | async-done | bytes 33554448 | tf_op jit(solution)/shard_map/all_gather | solution.py:11
  208.9 136.5 %while.13 = (s32[]{:T(128)}, f32[8,128,128]{1,2,0:T(8,128)S(1)}, s32[]{:T(128)}, f32[64,8,128,128]{3,2,1,0:T(8,128)}, s32[]{:T(128)}) while((s32[]{:T(128)}, f32[8,128,128]{1,2,0:T(8,128)S(1)}, s32[]{:T(128)}, f32[64,8,128,128]{3,2,1,0:T(8,128)}, s32[]{:T(128)}) %tuple.48), condition=%wide.region_2.3_spmd, body=%wide.region_1.2_spmd.sunk | while | flops 201457664 | bytes 3145811 | solution.py:19
  208.9 2.1 fusion.247
  219.6 2.1 fusion.247
  230.3 2.1 fusion.247
  238.8 2.1 fusion.247
  240.9 2.1 fusion.247
  249.5 2.1 fusion.247
  260.1 2.1 fusion.247
  268.7 2.1 fusion.247
  279.3 2.1 fusion.247
  285.7 2.1 fusion.247
  287.8 2.1 fusion.247
  298.5 2.1 fusion.247
  304.9 2.1 fusion.247
  307.0 2.1 fusion.247
  317.7 2.1 fusion.247
  324.1 2.1 fusion.247
  326.2 2.1 fusion.247
  336.9 2.1 fusion.247
  343.3 2.1 fusion.247
  (210 shorter events, 122.1 us)
Async XLA Ops:
  7.2 31.0 %all-gather.4.cloned.1.call-start = ((), (), s32[]{:S(2)}) async-start(), calls=%async_computation | async-start | bytes 1310720 | tf_op jit(solution)/shard_map/all_gather | solution.py:75
  7.9 201.0 %all-gather.6.cloned.1.call-start = ((), (), s32[]{:S(2)}) async-start(), calls=%async_computation.1 | async-start | bytes 34078720 | tf_op jit(solution)/shard_map/all_gather | solution.py:11
  10.6 49.5 %copy-start = (bf16[128,8,128]{2,0,1:T(8,128)(2,1)}, bf16[128,8,128]{2,0,1:T(8,128)(2,1)S(1)}, u32[]{:S(2)}) copy-start(bf16[128,8,128]{2,0,1:T(8,128)(2,1)S(1)} %copy.41) | copy-start | bytes 786436
Sparse Core Ops, SparseCore 0:
  9.8 28.3 all-gather.3
  64.4 144.4 all-gather.5
where the time goes:
time: 358 us; the launch traced here: 355 us
  waiting for transfers between devices  170 us (47%)
  matrix products  160 us (45%)
  between operations  14.7 us (4%)
  local copies, waits for them, and re-layouts  7.25 us (2%)
    all_gather x1, waiting for transfers between devices, entering(): everything = lax.all_gather(array, axis)  142 us
    dot_general x64, matrix products, combine(): return jnp.einsum('hde,hef->hdf', earlier, later, precision=highest)  132 us
    all_gather x1, waiting for transfers between devices, body(): lax.all_gather(features, 'head', axis=1, tiled=True)  27.5 us
  transfers between devices with their start and end apart: 2, of which 2 were waited for; matrix products, arithmetic and copies ran while one was open for 2% of the time, Pallas kernels for 0%

commit v1 on v0

--- a/solution.py
+++ b/solution.py
@@ -71,10 +71,46 @@
     tok_rows = query_vectors.shape[0]
     width = proj_weight.shape[1]
     local_heads = width // HEAD_DIM
+
+    def _assign_node(incoming_x, mesh_ax, where_dim=1):
+        carry_out, plain, view_out = (
+            lax.axis_size(mesh_ax),
+            lax.axis_index(mesh_ax),
+            incoming_x.shape[where_dim],
+        )
+        kept_rows = []
+        for idx in range(carry_out):
+            kept_rows.append((idx, (idx + 1) % carry_out))
+        table = []
+        for idx in range(carry_out):
+            table.append((idx, (idx - 1) % carry_out))
+        d_next = jnp.zeros(
+            (
+                *incoming_x.shape[:where_dim],
+                carry_out * view_out,
+                *incoming_x.shape[where_dim + 1 :],
+            ),
+            incoming_x.dtype,
+        )
+        d_next = lax.dynamic_update_slice_in_dim(
+            d_next, incoming_x, plain * view_out, axis=where_dim
+        )
+        item_now = front = incoming_x
+        carry = carry_out // 2
+        for ix in range(1, carry + 1):
+            item_now = lax.ppermute(item_now, mesh_ax, kept_rows)
+            d_next = lax.dynamic_update_slice_in_dim(
+                d_next, item_now, (plain - ix) % carry_out * view_out, axis=where_dim
+            )
+            if ix < carry_out - carry:
+                front = lax.ppermute(front, mesh_ax, table)
+                d_next = lax.dynamic_update_slice_in_dim(
+                    d_next, front, (plain + ix) % carry_out * view_out, axis=where_dim
+                )
+        return d_next
+
     raw_proj = jnp.dot(
-        lax.all_gather(features, "head", axis=1, tiled=True),
-        proj_weight,
-        preferred_element_type=jnp.float32,
+        _assign_node(features, "head"), proj_weight, preferred_element_type=jnp.float32
     )
     raw_proj = raw_proj.reshape(tok_rows, local_heads, HEAD_DIM)
     directions = raw_proj * lax.rsqrt(jnp.sum(raw_proj * raw_proj, axis=-1, keepdims=True) + 1e-06)

time: 358 us -> 346 us (0.966)
  waiting for transfers between devices: 170 us -> 156 us
  starting transfers between devices: 0.08 us -> 3.67 us
    all_gather x1 -> x0, waiting for transfers between devices: 27.5 us -> none  [body(): lax.all_gather(features, 'head', axis=1, tiled=True)]
    ppermute x0 -> x3, waiting for transfers between devices: none -> 14.4 us  [the longest x2 14.4 us: _assign_node(): item_now = lax.ppermute(item_now, mesh_ax, kept_rows)]
    ppermute x0 -> x3, starting transfers between devices: none -> 3.64 us  [the longest x1 3.63 us: _assign_node(): front = lax.ppermute(front, mesh_ax, table)]
  transfers between devices with their start and end apart: 2 -> 4, of which waited for: 2 -> 3; matrix products, arithmetic and copies ran while one was open for 2% -> 1% of each run, Pallas kernels for 0% -> 0%
where the time goes in v1:
time: 346 us; the launch traced here: 343 us
  matrix products  160 us (46%)
  waiting for transfers between devices  156 us (45%)
  between operations  14.8 us (4%)
  local copies, waits for them, and re-layouts  5.56 us (2%)
  starting transfers between devices  3.67 us (1%)
    all_gather x1, waiting for transfers between devices, entering(): everything = lax.all_gather(array, axis)  141 us
    dot_general x64, matrix products, combine(): return jnp.einsum('hde,hef->hdf', earlier, later, precision=highest)  132 us
    ppermute x2, waiting for transfers between devices, _assign_node(): item_now = lax.ppermute(item_now, mesh_ax, kept_rows)  14.4 us
  transfers between devices with their start and end apart: 4, of which 3 were waited for; matrix products, arithmetic and copies ran while one was open for 1% of the time, Pallas kernels for 0%

profile of v1, /device:TPU:1, one launch (start us, length us, event | category | flops | bytes accessed | tf_op | source)
XLA Modules:
  0.0 343.2 jit_solution(2283358836869334327)
XLA Ops:
  7.2 3.6 %collective-permute-start.1 = (bf16[128,1024]{1,0:T(8,128)(2,1)}, bf16[128,1024]{1,0:T(8,128)(2,1)S(1)}, u32[]{:S(2)}, u32[]{:S(2)}) collective-permute-start(bf16[128,1024]{1,0:T(8,128)(2,1)} %param.6), channel_id=1, source_target_pairs={{0,3},{1,0},{2,1},{3,2},{4,7},{5,4},{6,5},{7,6},{8,11},{9,8},{10,9... | collective-permute-start | bytes 786440 | tf_op jit(solution)/shard_map/ppermute | solution.py:106
  11.1 8.1 %collective-permute-done = bf16[128,1024]{1,0:T(8,128)(2,1)S(1)} collective-permute-done((bf16[128,1024]{1,0:T(8,128)(2,1)}, bf16[128,1024]{1,0:T(8,128)(2,1)S(1)}, u32[]{:S(2)}, u32[]{:S(2)}) %collective-permute-start) | collective-permute-done | bytes 262176 | tf_op jit(solution)/shard_map/ppermute | solution.py:101
  20.1 6.3 %collective-permute-done.2 = bf16[128,1024]{1,0:T(8,128)(2,1)S(1)} collective-permute-done((bf16[128,1024]{1,0:T(8,128)(2,1)S(1)}, bf16[128,1024]{1,0:T(8,128)(2,1)S(1)}, u32[]{:S(2)}, u32[]{:S(2)}) %collective-permute-start.2) | collective-permute-done | bytes 262176 | tf_op jit(solution)/shard_map/ppermute | solution.py:101
  26.5 4.7 %fusion.124 = f32[128,1024]{1,0:T(8,128)S(1)} fusion(bf16[128,4096]{1,0:T(8,128)(2,1)S(1)} %constant_dynamic-update-slice_fusion, bf16[4096,1024]{1,0:T(8,128)(2,1)} %param.7), kind=kOutput, calls=%fused_computation.189 | convolution fusion | flops 1073741824 | bytes 9961472 | tf_op jit(solution)/shard_map/dot_general | solution.py:112
  52.5 2.9 convolution_subtract_fusion
  55.4 141.5 %all-gather.3.cloned.1.call-done = f32[512,128,128]{2,1,0:T(8,128)} async-done(((f32[8,128,128]{2,1,0:T(8,128)}), f32[512,128,128]{2,1,0:T(8,128)}) %all-gather.3.cloned.1.call-update) | async-done | bytes 33554448 | tf_op jit(solution)/shard_map/all_gather | solution.py:11
  197.0 136.5 %while.13 = (s32[]{:T(128)}, f32[8,128,128]{1,2,0:T(8,128)S(1)}, s32[]{:T(128)}, f32[64,8,128,128]{3,2,1,0:T(8,128)}, s32[]{:T(128)}) while((s32[]{:T(128)}, f32[8,128,128]{1,2,0:T(8,128)S(1)}, s32[]{:T(128)}, f32[64,8,128,128]{3,2,1,0:T(8,128)}, s32[]{:T(128)}) %tuple.46), condition=%wide.region_2.3_spmd, body=%wide.region_1.2_spmd.sunk | while | flops 201457664 | bytes 3145811 | solution.py:19
  205.5 2.1 fusion.247
  211.9 2.1 fusion.247
  214.1 2.1 fusion.247
  224.7 2.1 fusion.247
  231.1 2.1 fusion.247
  233.3 2.1 fusion.247
  235.4 2.1 fusion.247
  243.9 2.1 fusion.247
  250.3 2.1 fusion.247
  254.6 2.1 fusion.247
  263.1 2.1 fusion.247
  269.5 2.1 fusion.247
  273.8 2.1 fusion.247
  280.2 2.1 fusion.247
  282.3 2.1 fusion.247
  288.7 2.1 fusion.247
  293.0 2.1 fusion.247
  (224 shorter events, 123.9 us)
Async XLA Ops:
  7.2 3.9 %copy-start.1 = (bf16[128,1024]{1,0:T(8,128)(2,1)S(1)}, bf16[128,1024]{1,0:T(8,128)(2,1)}, u32[]{:S(2)}) copy-start(bf16[128,1024]{1,0:T(8,128)(2,1)} %param.6) | copy-start | bytes 786436
  7.2 12.1 %copy-start.2 = (bf16[128,1024]{1,0:T(8,128)(2,1)S(1)}, bf16[128,1024]{1,0:T(8,128)(2,1)}, u32[]{:S(2)}) copy-start(bf16[128,1024]{1,0:T(8,128)(2,1)} %param.8) | copy-start | bytes 786436
  7.2 12.5 %copy-start.3 = (bf16[128,1024]{1,0:T(8,128)(2,1)S(1)}, bf16[128,1024]{1,0:T(8,128)(2,1)}, u32[]{:S(2)}) copy-start(bf16[128,1024]{1,0:T(8,128)(2,1)} %param.9) | copy-start | bytes 786436
  7.2 189.7 %all-gather.3.cloned.1.call-start = ((), (), s32[]{:S(2)}) async-start(), calls=%async_computation | async-start | bytes 34078720 | tf_op jit(solution)/shard_map/all_gather | solution.py:11
  7.2 12.8 %collective-permute-start.1 = (bf16[128,1024]{1,0:T(8,128)(2,1)}, bf16[128,1024]{1,0:T(8,128)(2,1)S(1)}, u32[]{:S(2)}, u32[]{:S(2)}) collective-permute-start(bf16[128,1024]{1,0:T(8,128)(2,1)} %param.6), channel_id=1, source_target_pairs={{0,3},{1,0},{2,1},{3,2},{4,7},{5,4},{6,5},{7,6},{8,11},{9,8},{10,9... | collective-permute-start | bytes 786440 | tf_op jit(solution)/shard_map/ppermute | solution.py:106
  10.9 8.3 %collective-permute-start = (bf16[128,1024]{1,0:T(8,128)(2,1)}, bf16[128,1024]{1,0:T(8,128)(2,1)S(1)}, u32[]{:S(2)}, u32[]{:S(2)}) collective-permute-start(bf16[128,1024]{1,0:T(8,128)(2,1)} %param.6), channel_id=1, source_target_pairs={{0,1},{1,2},{2,3},{3,0},{4,5},{5,6},{6,7},{7,4},{8,9},{9,10},{10,1... | collective-permute-start | bytes 786440 | tf_op jit(solution)/shard_map/ppermute | solution.py:101
  19.2 7.3 %collective-permute-start.2 = (bf16[128,1024]{1,0:T(8,128)(2,1)S(1)}, bf16[128,1024]{1,0:T(8,128)(2,1)S(1)}, u32[]{:S(2)}, u32[]{:S(2)}) collective-permute-start(bf16[128,1024]{1,0:T(8,128)(2,1)S(1)} %collective-permute-done), channel_id=1, source_target_pairs={{0,1},{1,2},{2,3},{3,0},{4,5},{5,6},{6,7},{7,4},{8,9},{9,10},{10,1... | collective-permute-start | bytes 786440 | tf_op jit(solution)/shard_map/ppermute | solution.py:101
  20.0 28.1 %copy-start = (bf16[128,8,128]{2,0,1:T(8,128)(2,1)}, bf16[128,8,128]{2,0,1:T(8,128)(2,1)S(1)}, u32[]{:S(2)}) copy-start(bf16[128,8,128]{2,0,1:T(8,128)(2,1)S(1)} %copy.41) | copy-start | bytes 786436
Sparse Core Ops, SparseCore 0:
  52.5 144.3 all-gather.2
